TPU v7x, 256 devices: a whole 4x4x8 slice. The times are simulated.
256 devices in a mesh: grp: 8 (over y_hi, x), dom: 32 (over y_lo, z, core).
Axes of the slice: x: 4, y: 4 (y_hi: 2, y_lo: 2; y = y_hi * 2 + y_lo), z: 8, core: 2. Of those that a mesh axis runs over, the one named last changes fastest.
Arguments:
- fine_matrix_blocks: bfloat16 [16384, 64, 768], P(('grp', 'dom')), may hold values from -0.21875 to 0.21875
- prolongator: bfloat16 [16384, 64, 64], P(('grp', 'dom')), may hold values from -1.5 to 1.5
- block_columns: int32 [16384, 12], P(('grp', 'dom')), may hold values from 0 to 16383, as said below
- block_aggregates: int32 [16384, 12], P(('grp', 'dom')), may hold values from 0 to 1023, as said below
- live_counts: int32 [256], P(('grp', 'dom')), may hold values from 16 to 64, as said below
Outputs:
- coarse_operator: float32 [1024, 64, 768], P('dom')
Inputs may be any that keep to these rules, and one draw needn't show every extreme that they name: live_counts[p] counts the first slots of partition p that hold block rows; some partition has 64 and some has 16. `block_columns`: entry 0 of row i is i itself. For a live row of partition p, every entry is a live row of partition p - 1, p or p + 1 (only partitions that exist); entries may repeat, and repeated blocks add. block_aggregates[i, k] is the aggregate of row block_columns[i, k]. Every row of partition p, with g = p // 32 and q = p % 32, has an aggregate from (((q + 4 * g) % 32) * 8 + g) * 4 to that number plus 4 - 1.
All inputs are finite; a program needn't handle non-finite values.
Results may differ from a plain program's by a relative error of at most 0.0029.
Values may be sent and summed in bfloat16 or wider, within the bound.
No kernel may reach another device: no remote copies, remote signals or barrier semaphores. Data moves between devices by JAX's collectives and lax.ppermute only.
A program may use at most 192 MiB of HBM per device.

v0:
```python
import jax
import jax.numpy as jnp
from jax import lax
from jax.sharding import PartitionSpec as P

AGG_DEV = 4


def extended(block, sides, width):
    for axis, dim in sides:
        count = lax.axis_size(axis)
        forward = [(i, i + 1) for i in range(count - 1)]
        backward = [(target, source) for source, target in forward]
        low = lax.ppermute(
            lax.slice_in_dim(block, block.shape[dim] - width, None, axis=dim), axis, forward
        )
        high = lax.ppermute(lax.slice_in_dim(block, 0, width, axis=dim), axis, backward)
        block = jnp.concatenate([low, block, high], axis=dim)
    return block


def passed_along(value, axis, by):
    peers = lax.axis_size(axis)
    return lax.ppermute(value, axis, [(i, (i + by) % peers) for i in range(peers)])


def local(fine_matrix_blocks, prolongator, block_columns, block_aggregates, live_counts):
    capacity = fine_matrix_blocks.shape[0]
    block_width = prolongator.shape[1]
    row_blocks = block_columns.shape[1]
    slot_width = 3 * AGG_DEV
    position = lax.axis_index(("grp", "dom"))
    ghosts = extended(prolongator, ((("grp", "dom"), 0),), capacity)
    local_rows = block_columns - (position - 1) * capacity
    gathered = jnp.take(ghosts, local_rows, axis=0)
    matrix_view = fine_matrix_blocks.reshape(capacity, block_width, row_blocks, block_width)
    products = jnp.einsum(
        "ixky,ikyz->ixkz", matrix_view, gathered, preferred_element_type=jnp.float32
    )
    coarse_slot = AGG_DEV * (local_rows // capacity) + block_aggregates % AGG_DEV
    live_rows = jnp.arange(capacity) < live_counts[0]
    slot_select = (coarse_slot[:, :, None] == jnp.arange(slot_width)[None, None, :]) & live_rows[
        :, None, None
    ]
    row_sums = jnp.einsum(
        "ikt,ixkz->ixtz", slot_select.astype(jnp.float32), products, precision=lax.Precision.HIGHEST
    )
    row_sums = row_sums.astype(jnp.bfloat16).reshape(
        capacity * block_width, slot_width * block_width
    )
    row_select = (block_aggregates[:, 0:1] % AGG_DEV == jnp.arange(AGG_DEV)[None, :]) & live_rows[
        :, None
    ]
    spread = row_select.astype(jnp.bfloat16)[:, None, :, None] * prolongator[:, :, None, :]
    spread = spread.reshape(capacity * block_width, AGG_DEV * block_width)
    coarse = lax.dot_general(
        spread, row_sums, (((0,), (0,)), ((), ())), preferred_element_type=jnp.float32
    )
    groups_count = lax.axis_size("grp")
    step_stride = lax.axis_size("dom") // groups_count
    group_index = lax.axis_index("grp")
    rotated = coarse
    for bit_number in range(groups_count.bit_length() - 1):
        arrived = passed_along(rotated, "dom", step_stride << bit_number)
        rotated = jnp.where((group_index >> bit_number) % 2 == 1, arrived, rotated)
    result = lax.all_gather(rotated[None], "grp", axis=0, tiled=True)
    return result.reshape(groups_count * AGG_DEV, block_width, slot_width * block_width)


def solution(mesh):
    return jax.shard_map(
        local,
        mesh=mesh,
        in_specs=(
            P(("grp", "dom"), None, None),
            P(("grp", "dom"), None, None),
            P(("grp", "dom"), None),
            P(("grp", "dom"), None),
            P(("grp", "dom")),
        ),
        out_specs=P("dom", None, None),
        check_vma=False,
    )
```

profile of v0, /device:TPU:1, one launch (start us, length us, event | category | flops | bytes accessed | tf_op | source)
XLA Modules:
  0.0 395.2 jit_solution(863986176305773852)
XLA Ops:
  6.5 0.0 copy-start.1
  6.5 0.0 all-gather.3.cloned.1.call-start
  6.5 5.0 %collective-permute-start = (bf16[64,64,64]{2,1,0:T(8,128)(2,1)}, bf16[64,64,64]{2,1,0:T(8,128)(2,1)S(1)}, u32[]{:S(2)}, u32[]{:S(2)}) collective-permute-start(bf16[64,64,64]{2,1,0:T(8,128)(2,1)} %param.6), channel_id=1, source_target_pairs={{0,1},{1,2},{2,3},{3,4},{4,5},{5,6},{6,7},{7,8},{8,9},{9,10},{10,1... | collective-permute-start | bytes 1572872 | tf_op jit(solution)/shard_map/ppermute | solution.py:14
  11.6 1.9 collective-permute-start.1
  13.5 0.7 compare_and_fusion
  14.2 0.7 fusion.17
  15.0 0.7 fusion.22
  15.7 0.1 copy.14
  15.8 0.1 reshape.79
  15.9 0.1 copy.13
  16.0 19.7 %reshape.74 = bf16[64,64,12,64]{3,2,1,0:T(8,128)(2,1)} reshape(bf16[64,64,768]{2,1,0:T(8,128)(2,1)} %param.5) | data formatting | bytes 12582912 | tf_op jit(solution)/shard_map/reshape | solution.py:36
  35.7 0.1 copy.17
  36.4 0.1 copy.12
  36.5 0.0 copy-done.1
  36.6 4.2 %broadcast_multiply_fusion = bf16[64,64,4,64]{3,2,1,0:T(4,128)(2,1)} fusion(bf16[64,64,64]{2,1,0:T(8,128)(2,1)S(1)} %copy-done.1, bf16[64,4]{1,0:T(8,128)(2,1)S(1)} %copy.12), kind=kLoop, calls=%fused_computation.9 | loop fusion | flops 1048576 | bytes 2621952 | tf_op jit(solution)/shard_map/mul | solution.py:54
  40.8 7.0 %mul.38 = bf16[4096,256]{1,0:T(8,128)(2,1)} reshape(bf16[64,64,4,64]{3,2,1,0:T(4,128)(2,1)} %broadcast_multiply_fusion) | data formatting | bytes 4194304 | tf_op jit(solution)/shard_map/mul | solution.py:54
  47.7 0.0 collective-permute-done
  47.8 0.0 copy-start.2
  47.8 1.0 copy-done.2
  48.7 0.0 collective-permute-done.1
  48.7 2.2 pad_maximum_fusion
  51.0 18.2 %gather_fusion = bf16[768,64,64]{2,1,0:T(8,128)(2,1)} fusion(bf16[192,64,64]{2,1,0:T(8,128)(2,1)S(1)} %pad_maximum_fusion, s32[1024]{0:T(1024)S(1)} %pad_clamp_fusion), kind=kCustom, calls=%fused_computation | custom fusion | bytes 12585984 | tf_op jit(solution)/shard_map/jit(_take)/gather | solution.py:35
  69.1 16.6 %copy.15 = bf16[64,12,64,64]{2,3,1,0:T(8,128)(2,1)} copy(bf16[64,12,64,64]{3,2,1,0:T(8,128)(2,1)} %bitcast.18) | data formatting | bytes 12582912 | tf_op jit(solution)/shard_map/jit(_take)/gather | solution.py:35
  85.8 21.7 %fusion.4 = f32[64,64,12,64]{1,3,2,0:T(8,128)} fusion(bf16[64,64,12,64]{3,2,1,0:T(8,128)(2,1)} %reshape.74, bf16[64,12,64,64]{2,3,1,0:T(8,128)(2,1)} %copy.15, pred[64,12]{1,0:T(8,128)(4,1)S(1)} %copy.13), kind=kOutput, calls=%fused_computation.6 | convolution fusion | flops 405798912 | bytes 25166592 | tf_op jit(solution)/shard_map/ixky,ikyz->ixkz/dot_general | solution.py:37
  107.5 31.1 %copy.18 = f32[64,64,12,64]{3,2,1,0:T(8,128)} copy(f32[64,64,12,64]{1,3,2,0:T(8,128)} %fusion.4) | data formatting | bytes 25165824 | tf_op jit(solution)/shard_map/ixky,ikyz->ixkz/transpose | solution.py:37
  138.6 25.0 %convert_bitcast_fusion = bf16[64,64,12,64]{3,2,1,0:T(8,128)(2,1)} fusion(f32[64,64,12,64]{3,2,1,0:T(8,128)} %copy.18, s32[64,12]{1,0:T(8,128)S(1)} %copy.17, pred[64]{0:T(512)(128)(4,1)S(1)} %iota_compare_fusion.2), kind=kOutput, calls=%fused_computation.1 | convolution fusion | flops 456148992 | bytes 18877504 | tf_op jit(solution)/shard_map/ikt,ixkz->ixtz/dot_general | solution.py:45
  163.5 0.0 copy-start
  163.5 20.9 %reshape.90 = bf16[4096,768]{1,0:T(8,128)(2,1)} reshape(bf16[64,64,12,64]{3,2,1,0:T(8,128)(2,1)} %convert_bitcast_fusion) | data formatting | bytes 12582912 | tf_op jit(solution)/shard_map/reshape | solution.py:48
  184.4 0.0 copy-done
  184.4 4.6 %fusion.25 = f32[256,768]{1,0:T(8,128)S(1)} fusion(bf16[4096,256]{1,0:T(8,128)(2,1)S(1)} %copy-done, bf16[4096,768]{1,0:T(8,128)(2,1)} %reshape.90), kind=kOutput, calls=%fused_computation.44 | convolution fusion | flops 1610612736 | bytes 9175040 | tf_op jit(solution)/shard_map/dot_general | solution.py:56
  189.0 3.3 collective-permute-start.2
  192.3 36.2 %collective-permute-done.2 = f32[256,768]{1,0:T(8,128)S(1)} collective-permute-done((f32[256,768]{1,0:T(8,128)S(1)}, f32[256,768]{1,0:T(8,128)S(1)}, u32[]{:S(2)}, u32[]{:S(2)}) %collective-permute-start.2) | collective-permute-done | bytes 786464 | tf_op jit(solution)/shard_map/ppermute | solution.py:24
  228.5 0.1 broadcast_select_fusion
  228.6 0.1 collective-permute-start.3
  228.7 39.8 %collective-permute-done.3 = f32[256,768]{1,0:T(8,128)S(1)} collective-permute-done((f32[256,768]{1,0:T(8,128)S(1)}, f32[256,768]{1,0:T(8,128)S(1)}, u32[]{:S(2)}, u32[]{:S(2)}) %collective-permute-start.3) | collective-permute-done | bytes 786464 | tf_op jit(solution)/shard_map/ppermute | solution.py:24
  268.6 0.1 broadcast_select_fusion.1
  268.7 0.1 collective-permute-start.4
  268.8 17.5 %collective-permute-done.4 = f32[256,768]{1,0:T(8,128)S(1)} collective-permute-done((f32[256,768]{1,0:T(8,128)S(1)}, f32[256,768]{1,0:T(8,128)S(1)}, u32[]{:S(2)}, u32[]{:S(2)}) %collective-permute-start.4) | collective-permute-done | bytes 786464 | tf_op jit(solution)/shard_map/ppermute | solution.py:24
  286.3 1.0 broadcast_select_fusion.2
  287.3 0.0 all-gather.3.cloned.1.call-update
  287.3 94.9 %all-gather.3.cloned.1.call-done = f32[2048,768]{1,0:T(8,128)} async-done(((f32[256,768]{1,0:T(8,128)}), f32[2048,768]{1,0:T(8,128)}) %all-gather.3.cloned.1.call-update) | async-done | bytes 6291472 | tf_op jit(solution)/shard_map/all_gather | solution.py:66
  382.2 6.2 %copy.28 = f32[32,64,768]{2,1,0:T(8,128)} copy(f32[32,64,768]{2,1,0:T(8,128)} %bitcast.19) | data formatting | bytes 12582912
  (3 shorter events, 0.0 us)
Async XLA Ops:
  6.5 30.0 %copy-start.1 = (bf16[64,64,64]{2,1,0:T(8,128)(2,1)S(1)}, bf16[64,64,64]{2,1,0:T(8,128)(2,1)}, u32[]{:S(2)}) copy-start(bf16[64,64,64]{2,1,0:T(8,128)(2,1)} %param.6) | copy-start | bytes 1572868
  6.5 375.7 %all-gather.3.cloned.1.call-start = ((), (), s32[]{:S(2)}) async-start(), calls=%async_computation | async-start | bytes 7077888 | tf_op jit(solution)/shard_map/all_gather | solution.py:66
  6.5 41.2 %collective-permute-start = (bf16[64,64,64]{2,1,0:T(8,128)(2,1)}, bf16[64,64,64]{2,1,0:T(8,128)(2,1)S(1)}, u32[]{:S(2)}, u32[]{:S(2)}) collective-permute-start(bf16[64,64,64]{2,1,0:T(8,128)(2,1)} %param.6), channel_id=1, source_target_pairs={{0,1},{1,2},{2,3},{3,4},{4,5},{5,6},{6,7},{7,8},{8,9},{9,10},{10,1... | collective-permute-start | bytes 1572872 | tf_op jit(solution)/shard_map/ppermute | solution.py:14
  11.6 37.1 %collective-permute-start.1 = (bf16[64,64,64]{2,1,0:T(8,128)(2,1)}, bf16[64,64,64]{2,1,0:T(8,128)(2,1)}, u32[]{:S(2)}, u32[]{:S(2)}) collective-permute-start(bf16[64,64,64]{2,1,0:T(8,128)(2,1)} %param.6), channel_id=1, source_target_pairs={{1,0},{2,1},{3,2},{4,3},{5,4},{6,5},{7,6},{8,7},{9,8},{10,9},{11,1... | collective-permute-start | bytes 1572872 | tf_op jit(solution)/shard_map/ppermute | solution.py:17
  47.8 1.0 copy-start.2
  163.5 20.9 %copy-start = (bf16[4096,256]{1,0:T(8,128)(2,1)S(1)}, bf16[4096,256]{1,0:T(8,128)(2,1)}, u32[]{:S(2)}) copy-start(bf16[4096,256]{1,0:T(8,128)(2,1)} %mul.38) | copy-start | bytes 6291460
  189.0 39.5 %collective-permute-start.2 = (f32[256,768]{1,0:T(8,128)S(1)}, f32[256,768]{1,0:T(8,128)S(1)}, u32[]{:S(2)}, u32[]{:S(2)}) collective-permute-start(f32[256,768]{1,0:T(8,128)S(1)} %fusion.25), channel_id=1, source_target_pairs={{0,4},{1,5},{2,6},{3,7},{4,8},{5,9},{6,10},{7,11},{8,12},{9,13},{1... | collective-permute-start | bytes 2359304 | tf_op jit(solution)/shard_map/ppermute | solution.py:24
  228.6 39.9 %collective-permute-start.3 = (f32[256,768]{1,0:T(8,128)S(1)}, f32[256,768]{1,0:T(8,128)S(1)}, u32[]{:S(2)}, u32[]{:S(2)}) collective-permute-start(f32[256,768]{1,0:T(8,128)S(1)} %broadcast_select_fusion), channel_id=1, source_target_pairs={{0,8},{1,9},{2,10},{3,11},{4,12},{5,13},{6,14},{7,15},{8,16},{9,17... | collective-permute-start | bytes 2359304 | tf_op jit(solution)/shard_map/ppermute | solution.py:24
  268.7 17.6 %collective-permute-start.4 = (f32[256,768]{1,0:T(8,128)S(1)}, f32[256,768]{1,0:T(8,128)S(1)}, u32[]{:S(2)}, u32[]{:S(2)}) collective-permute-start(f32[256,768]{1,0:T(8,128)S(1)} %broadcast_select_fusion.1), channel_id=1, source_target_pairs={{0,16},{1,17},{2,18},{3,19},{4,20},{5,21},{6,22},{7,23},{8,24},{9,... | collective-permute-start | bytes 2359304 | tf_op jit(solution)/shard_map/ppermute | solution.py:24
Sparse Core Ops, SparseCore 0:
  287.4 94.7 all-gather.2
where the time goes:
time: 398 us; the launch traced here: 395 us
  waiting for transfers between devices  188 us (47%)
  local copies, waits for them, and re-layouts  121 us (30%)
  matrix products  51.3 us (13%)
  between operations  14.2 us (4%)
  starting transfers between devices  10.4 us (3%)
  other arithmetic  9.74 us (2%)
    all_gather x1, waiting for transfers between devices, local(): result = lax.all_gather(rotated[None], 'grp', axis=0, tiled=True)  94.9 us
    ppermute x3, waiting for transfers between devices, passed_along(): lax.ppermute(value, axis, [(i, (i + by) % peers) for i in range(peers)])  93.6 us
    gather x2, local copies, waits for them, and re-layouts, local(): gathered = jnp.take(ghosts, local_rows, axis=0)  34.8 us
    transpose x1, local copies, waits for them, and re-layouts, local(): jnp.einsum('ixky,ikyz->ixkz', matrix_view, gathered, preferred_element_ty...  31.1 us
    dot_general x1, matrix products, local(): jnp.einsum('ikt,ixkz->ixtz', slot_select.astype(jnp.float32), products, p...  25 us
    dot_general x1, matrix products, local(): jnp.einsum('ixky,ikyz->ixkz', matrix_view, gathered, preferred_element_ty...  21.7 us
    reshape x1, local copies, waits for them, and re-layouts, local(): row_sums.astype(jnp.bfloat16)  20.9 us
    reshape x1, local copies, waits for them, and re-layouts, local(): fine_matrix_blocks.reshape(capacity, block_width, row_blocks, block_width)  19.7 us
  transfers between devices with their start and end apart: 6, of which 4 were waited for; matrix products, arithmetic and copies ran while one was open for 8% of the time, Pallas kernels for 0%

commit v1 on v0

--- a/solution.py
+++ b/solution.py
@@ -63,7 +63,9 @@
     for bit_number in range(groups_count.bit_length() - 1):
         arrived = passed_along(rotated, "dom", step_stride << bit_number)
         rotated = jnp.where((group_index >> bit_number) % 2 == 1, arrived, rotated)
-    result = lax.all_gather(rotated[None], "grp", axis=0, tiled=True)
+    block_2 = rotated[None]
+    sent = jnp.stack([block_2] * lax.axis_size("grp"))
+    result = jnp.concatenate(lax.all_to_all(sent, "grp", 0, 0), axis=0)
     return result.reshape(groups_count * AGG_DEV, block_width, slot_width * block_width)
 
 

time: 398 us -> 368 us (0.925)
  the two profiles are of different devices: /device:TPU:1 before, /device:TPU:32 now
where the time goes in v1:
time: 368 us; the launch traced here: 365 us
  local copies, waits for them, and re-layouts  118 us (32%)
  waiting for transfers between devices  85.7 us (23%)
  blocking collectives  80 us (22%)
  matrix products  51.3 us (14%)
  starting transfers between devices  20.3 us (6%)
  other arithmetic  8.86 us (2%)
    ppermute x3, waiting for transfers between devices, passed_along(): lax.ppermute(value, axis, [(i, (i + by) % peers) for i in range(peers)])  85.7 us
    all_to_all x1, blocking collectives, local(): result = jnp.concatenate(lax.all_to_all(sent, 'grp', 0, 0), axis=0)  80 us
    gather x2, local copies, waits for them, and re-layouts, local(): gathered = jnp.take(ghosts, local_rows, axis=0)  34.8 us
    transpose x1, local copies, waits for them, and re-layouts, local(): jnp.einsum('ixky,ikyz->ixkz', matrix_view, gathered, preferred_element_ty...  31.1 us
    dot_general x1, matrix products, local(): jnp.einsum('ikt,ixkz->ixtz', slot_select.astype(jnp.float32), products, p...  25 us
    dot_general x1, matrix products, local(): jnp.einsum('ixky,ikyz->ixkz', matrix_view, gathered, preferred_element_ty...  21.7 us
    reshape x1, local copies, waits for them, and re-layouts, local(): row_sums.astype(jnp.bfloat16)  20.9 us
    reshape x1, local copies, waits for them, and re-layouts, local(): fine_matrix_blocks.reshape(capacity, block_width, row_blocks, block_width)  19.7 us
  transfers between devices with their start and end apart: 5, of which 3 were waited for; matrix products, arithmetic and copies ran while one was open for 9% of the time, Pallas kernels for 0%

profile of v1, /device:TPU:32, one launch (start us, length us, event | category | flops | bytes accessed | tf_op | source)
XLA Modules:
  0.0 365.0 jit_solution(12219956924152378064)
XLA Ops:
  0.0 0.0 copy-start.1
  0.0 2.0 collective-permute-start
  2.1 3.6 collective-permute-start.1
  5.7 0.7 compare_and_fusion
  6.4 0.7 fusion.17
  7.2 0.7 fusion.22
  7.8 0.1 copy.21
  7.9 0.1 reshape.77
  8.0 0.1 copy.20
  8.2 19.7 %reshape.73 = bf16[64,64,12,64]{3,2,1,0:T(8,128)(2,1)} reshape(bf16[64,64,768]{2,1,0:T(8,128)(2,1)} %param.5) | data formatting | bytes 12582912 | tf_op jit(solution)/shard_map/reshape | solution.py:36
  27.9 0.1 copy.24
  28.6 0.1 copy.19
  28.8 0.0 copy-done.1
  28.8 4.2 %broadcast_multiply_fusion = bf16[64,64,4,64]{3,2,1,0:T(4,128)(2,1)} fusion(bf16[64,64,64]{2,1,0:T(8,128)(2,1)S(1)} %copy-done.1, bf16[64,4]{1,0:T(8,128)(2,1)S(1)} %copy.19), kind=kLoop, calls=%fused_computation.9 | loop fusion | flops 1048576 | bytes 2621952 | tf_op jit(solution)/shard_map/mul | solution.py:54
  33.0 7.0 %mul.38 = bf16[4096,256]{1,0:T(8,128)(2,1)} reshape(bf16[64,64,4,64]{3,2,1,0:T(4,128)(2,1)} %broadcast_multiply_fusion) | data formatting | bytes 4194304 | tf_op jit(solution)/shard_map/mul | solution.py:54
  40.0 0.0 collective-permute-done
  40.0 0.0 copy-start.2
  40.0 1.0 copy-done.2
  40.9 0.0 collective-permute-done.1
  40.9 2.2 pad_maximum_fusion
  43.2 18.2 %gather_fusion = bf16[768,64,64]{2,1,0:T(8,128)(2,1)} fusion(bf16[192,64,64]{2,1,0:T(8,128)(2,1)S(1)} %pad_maximum_fusion, s32[1024]{0:T(1024)S(1)} %pad_clamp_fusion), kind=kCustom, calls=%fused_computation | custom fusion | bytes 12585984 | tf_op jit(solution)/shard_map/jit(_take)/gather | solution.py:35
  61.3 16.6 %copy.22 = bf16[64,12,64,64]{2,3,1,0:T(8,128)(2,1)} copy(bf16[64,12,64,64]{3,2,1,0:T(8,128)(2,1)} %bitcast.18) | data formatting | bytes 12582912 | tf_op jit(solution)/shard_map/jit(_take)/gather | solution.py:35
  78.0 21.7 %fusion.4 = f32[64,64,12,64]{1,3,2,0:T(8,128)} fusion(bf16[64,64,12,64]{3,2,1,0:T(8,128)(2,1)} %reshape.73, bf16[64,12,64,64]{2,3,1,0:T(8,128)(2,1)} %copy.22, pred[64,12]{1,0:T(8,128)(4,1)S(1)} %copy.20), kind=kOutput, calls=%fused_computation.6 | convolution fusion | flops 405798912 | bytes 25166592 | tf_op jit(solution)/shard_map/ixky,ikyz->ixkz/dot_general | solution.py:37
  99.7 31.1 %copy.25 = f32[64,64,12,64]{3,2,1,0:T(8,128)} copy(f32[64,64,12,64]{1,3,2,0:T(8,128)} %fusion.4) | data formatting | bytes 25165824 | tf_op jit(solution)/shard_map/ixky,ikyz->ixkz/transpose | solution.py:37
  130.8 25.0 %convert_bitcast_fusion = bf16[64,64,12,64]{3,2,1,0:T(8,128)(2,1)} fusion(f32[64,64,12,64]{3,2,1,0:T(8,128)} %copy.25, s32[64,12]{1,0:T(8,128)S(1)} %copy.24, pred[64]{0:T(512)(128)(4,1)S(1)} %iota_compare_fusion.2), kind=kOutput, calls=%fused_computation.1 | convolution fusion | flops 456148992 | bytes 18877504 | tf_op jit(solution)/shard_map/ikt,ixkz->ixtz/dot_general | solution.py:45
  155.8 0.0 copy-start
  155.8 20.9 %reshape.86 = bf16[4096,768]{1,0:T(8,128)(2,1)} reshape(bf16[64,64,12,64]{3,2,1,0:T(8,128)(2,1)} %convert_bitcast_fusion) | data formatting | bytes 12582912 | tf_op jit(solution)/shard_map/reshape | solution.py:48
  176.7 0.0 copy-done
  176.7 4.6 %fusion.25 = f32[256,768]{1,0:T(8,128)S(1)} fusion(bf16[4096,256]{1,0:T(8,128)(2,1)S(1)} %copy-done, bf16[4096,768]{1,0:T(8,128)(2,1)} %reshape.86), kind=kOutput, calls=%fused_computation.44 | convolution fusion | flops 1610612736 | bytes 9175040 | tf_op jit(solution)/shard_map/dot_general | solution.py:56
  181.3 3.6 collective-permute-start.2
  184.8 34.8 %collective-permute-done.2 = f32[256,768]{1,0:T(8,128)S(1)} collective-permute-done((f32[256,768]{1,0:T(8,128)S(1)}, f32[256,768]{1,0:T(8,128)S(1)}, u32[]{:S(2)}, u32[]{:S(2)}) %collective-permute-start.2) | collective-permute-done | bytes 786464 | tf_op jit(solution)/shard_map/ppermute | solution.py:24
  219.7 0.1 broadcast_select_fusion
  219.7 5.0 %collective-permute-start.3 = (f32[256,768]{1,0:T(8,128)S(1)}, f32[256,768]{1,0:T(8,128)S(1)}, u32[]{:S(2)}, u32[]{:S(2)}) collective-permute-start(f32[256,768]{1,0:T(8,128)S(1)} %broadcast_select_fusion), channel_id=1, source_target_pairs={{0,8},{1,9},{2,10},{3,11},{4,12},{5,13},{6,14},{7,15},{8,16},{9,17... | collective-permute-start | bytes 2359304 | tf_op jit(solution)/shard_map/ppermute | solution.py:24
  224.7 33.2 %collective-permute-done.3 = f32[256,768]{1,0:T(8,128)S(1)} collective-permute-done((f32[256,768]{1,0:T(8,128)S(1)}, f32[256,768]{1,0:T(8,128)S(1)}, u32[]{:S(2)}, u32[]{:S(2)}) %collective-permute-start.3) | collective-permute-done | bytes 786464 | tf_op jit(solution)/shard_map/ppermute | solution.py:24
  258.0 0.1 broadcast_select_fusion.1
  258.1 6.1 %collective-permute-start.4 = (f32[256,768]{1,0:T(8,128)S(1)}, f32[256,768]{1,0:T(8,128)S(1)}, u32[]{:S(2)}, u32[]{:S(2)}) collective-permute-start(f32[256,768]{1,0:T(8,128)S(1)} %broadcast_select_fusion.1), channel_id=1, source_target_pairs={{0,16},{1,17},{2,18},{3,19},{4,20},{5,21},{6,22},{7,23},{8,24},{9,... | collective-permute-start | bytes 2359304 | tf_op jit(solution)/shard_map/ppermute | solution.py:24
  264.1 17.6 %collective-permute-done.4 = f32[256,768]{1,0:T(8,128)S(1)} collective-permute-done((f32[256,768]{1,0:T(8,128)S(1)}, f32[256,768]{1,0:T(8,128)S(1)}, u32[]{:S(2)}, u32[]{:S(2)}) %collective-permute-start.4) | collective-permute-done | bytes 786464 | tf_op jit(solution)/shard_map/ppermute | solution.py:24
  281.7 0.1 broadcast_select_fusion.2
  281.8 0.5 stack.3
  282.4 80.0 %all_to_all.5 = f32[8,1,256,768]{3,2,1,0:T(8,128)S(1)} all-to-all(f32[8,1,256,768]{3,2,1,0:T(8,128)S(1)} %stack.3), channel_id=1, replica_groups=mesh['grp'=8,'dom'=32] {'grp'}, dimensions={0} | all-to-all | bytes 12582912 | tf_op jit(solution)/shard_map/all_to_all | solution.py:68
  362.3 2.7 copy.35
  (3 shorter events, 0.0 us)
Async XLA Ops:
  0.0 28.8 %copy-start.1 = (bf16[64,64,64]{2,1,0:T(8,128)(2,1)S(1)}, bf16[64,64,64]{2,1,0:T(8,128)(2,1)}, u32[]{:S(2)}) copy-start(bf16[64,64,64]{2,1,0:T(8,128)(2,1)} %param.6) | copy-start | bytes 1572868
  0.0 40.0 %collective-permute-start = (bf16[64,64,64]{2,1,0:T(8,128)(2,1)}, bf16[64,64,64]{2,1,0:T(8,128)(2,1)S(1)}, u32[]{:S(2)}, u32[]{:S(2)}) collective-permute-start(bf16[64,64,64]{2,1,0:T(8,128)(2,1)} %param.6), channel_id=1, source_target_pairs={{0,1},{1,2},{2,3},{3,4},{4,5},{5,6},{6,7},{7,8},{8,9},{9,10},{10,1... | collective-permute-start | bytes 1572872 | tf_op jit(solution)/shard_map/ppermute | solution.py:14
  2.1 38.9 %collective-permute-start.1 = (bf16[64,64,64]{2,1,0:T(8,128)(2,1)}, bf16[64,64,64]{2,1,0:T(8,128)(2,1)}, u32[]{:S(2)}, u32[]{:S(2)}) collective-permute-start(bf16[64,64,64]{2,1,0:T(8,128)(2,1)} %param.6), channel_id=1, source_target_pairs={{1,0},{2,1},{3,2},{4,3},{5,4},{6,5},{7,6},{8,7},{9,8},{10,9},{11,1... | collective-permute-start | bytes 1572872 | tf_op jit(solution)/shard_map/ppermute | solution.py:17
  40.0 1.0 copy-start.2
  155.8 20.9 %copy-start = (bf16[4096,256]{1,0:T(8,128)(2,1)S(1)}, bf16[4096,256]{1,0:T(8,128)(2,1)}, u32[]{:S(2)}) copy-start(bf16[4096,256]{1,0:T(8,128)(2,1)} %mul.38) | copy-start | bytes 6291460
  181.3 38.4 %collective-permute-start.2 = (f32[256,768]{1,0:T(8,128)S(1)}, f32[256,768]{1,0:T(8,128)S(1)}, u32[]{:S(2)}, u32[]{:S(2)}) collective-permute-start(f32[256,768]{1,0:T(8,128)S(1)} %fusion.25), channel_id=1, source_target_pairs={{0,4},{1,5},{2,6},{3,7},{4,8},{5,9},{6,10},{7,11},{8,12},{9,13},{1... | collective-permute-start | bytes 2359304 | tf_op jit(solution)/shard_map/ppermute | solution.py:24
  219.7 38.2 %collective-permute-start.3 = (f32[256,768]{1,0:T(8,128)S(1)}, f32[256,768]{1,0:T(8,128)S(1)}, u32[]{:S(2)}, u32[]{:S(2)}) collective-permute-start(f32[256,768]{1,0:T(8,128)S(1)} %broadcast_select_fusion), channel_id=1, source_target_pairs={{0,8},{1,9},{2,10},{3,11},{4,12},{5,13},{6,14},{7,15},{8,16},{9,17... | collective-permute-start | bytes 2359304 | tf_op jit(solution)/shard_map/ppermute | solution.py:24
  258.1 23.7 %collective-permute-start.4 = (f32[256,768]{1,0:T(8,128)S(1)}, f32[256,768]{1,0:T(8,128)S(1)}, u32[]{:S(2)}, u32[]{:S(2)}) collective-permute-start(f32[256,768]{1,0:T(8,128)S(1)} %broadcast_select_fusion.1), channel_id=1, source_target_pairs={{0,16},{1,17},{2,18},{3,19},{4,20},{5,21},{6,22},{7,23},{8,24},{9,... | collective-permute-start | bytes 2359304 | tf_op jit(solution)/shard_map/ppermute | solution.py:24
